TPU v7x, 256 devices: a whole 4x4x8 slice. The times are simulated.
256 devices in a mesh: row: 32 (over z, x_lo, core), col: 8 (over y, x_hi).
Axes of the slice: x: 4 (x_hi: 2, x_lo: 2; x = x_hi * 2 + x_lo), y: 4, z: 8, core: 2. Of those that a mesh axis runs over, the one named last changes fastest.
Arguments:
- grad_out: bfloat16 [4096, 8192], P('row', 'col'), may hold values from -6 to 6
- weight: bfloat16 [28672, 8192], P('row', 'col'), may hold values from -0.0625 to 0.0625
Outputs:
- grad_in: bfloat16 [4096, 28672], P('col', 'row')
All inputs are finite; a program needn't handle non-finite values.
Results may differ from a plain program's by a relative error of at most 0.015.
Values may be sent and summed in bfloat16 or wider, within the bound.
No kernel may reach another device: no remote copies, remote signals or barrier semaphores. Data moves between devices by JAX's collectives and lax.ppermute only.
A program may use at most 128 MiB of HBM per device.

v0:
```python
import jax
import jax.numpy as jnp
from jax import lax
from jax.sharding import PartitionSpec as P


def contract_last(left_side, right_side):
    return lax.dot_general(
        left_side, right_side, (((1,), (1,)), ((), ())), preferred_element_type=jnp.float32
    )


def body(grad_out, weight):
    gathered = lax.all_gather(grad_out, "row", axis=0, tiled=True)
    rounded = lax.optimization_barrier(contract_last(gathered, weight).astype(jnp.bfloat16))
    return lax.psum_scatter(
        rounded.astype(jnp.float32).astype(jnp.bfloat16), "col", scatter_dimension=0, tiled=True
    )


def solution(mesh):
    in_specs = (P("row", "col"), P("row", "col"))
    out_specs = P("col", "row")
    return jax.shard_map(body, mesh=mesh, in_specs=in_specs, out_specs=out_specs, check_vma=False)
```

profile of v0, /device:TPU:1, one launch (start us, length us, event | category | flops | bytes accessed | tf_op | source)
XLA Modules:
  0.0 215.4 jit_solution(4067876337323269924)
XLA Ops:
  6.5 0.0 copy-start
  6.5 0.0 all-gather.2.cloned.1.call-start
  6.5 0.7 all-gather.2.cloned.1.call-update
  7.3 0.0 reduce-scatter.2.cloned.1.call-start
  7.3 77.8 %all-gather.2.cloned.1.call-done = bf16[4096,1024]{1,0:T(8,128)(2,1)} async-done(((bf16[128,1024]{1,0:T(8,128)(2,1)}), bf16[4096,1024]{1,0:T(8,128)(2,1)}) %all-gather.2.cloned.1.call-update) | async-done | bytes 8388624 | tf_op jit(solution)/shard_map/all_gather | solution.py:14
  85.1 0.0 copy-done
  85.1 14.3 %convolution_convert_fusion = bf16[4096,896]{1,0:T(8,128)(2,1)} fusion(bf16[4096,1024]{1,0:T(8,128)(2,1)} %all-gather.2.cloned.1.call-done, bf16[896,1024]{1,0:T(8,128)(2,1)S(1)} %copy-done), kind=kOutput, calls=%fused_computation | convolution fusion | flops 7519862784 | bytes 17563648 | tf_op jit(solution)/shard_map/dot_general | solution.py:8
  99.4 0.0 reduce-scatter.2.cloned.1.call-update
  99.4 109.1 %reduce-scatter.2.cloned.1.call-done = bf16[512,896]{1,0:T(8,128)(2,1)} async-done(((bf16[4096,896]{1,0:T(8,128)(2,1)}), bf16[512,896]{1,0:T(8,128)(2,1)}) %reduce-scatter.2.cloned.1.call-update) | async-done | bytes 917520 | tf_op jit(solution)/shard_map/reduce_scatter | solution.py:16
Async XLA Ops:
  6.5 78.6 %copy-start = (bf16[896,1024]{1,0:T(8,128)(2,1)S(1)}, bf16[896,1024]{1,0:T(8,128)(2,1)}, u32[]{:S(2)}) copy-start(bf16[896,1024]{1,0:T(8,128)(2,1)} %param.3) | copy-start | bytes 5505028
  6.5 78.6 %all-gather.2.cloned.1.call-start = ((), (), s32[]{:S(2)}) async-start(), calls=%async_computation.1 | async-start | bytes 8650752 | tf_op jit(solution)/shard_map/all_gather | solution.py:14
  7.3 201.3 %reduce-scatter.2.cloned.1.call-start = ((), (), s32[]{:S(2)}) async-start(), calls=%async_computation.2 | async-start | bytes 8257536 | tf_op jit(solution)/shard_map/reduce_scatter | solution.py:16
Sparse Core Ops, SparseCore 0:
  9.2 75.8 all-gather.1
  99.6 108.9 reduce-scatter.1
where the time goes:
time: 215 us
  waiting for transfers between devices  188 us (87%)
  matrix products  14.3 us (7%)
  between operations  13.4 us (6%)
    reduce_scatter x1, waiting for transfers between devices, body(): lax.psum_scatter(rounded.astype(jnp.float32).astype(jnp.bfloat16), 'col',...  109 us
    all_gather x1, waiting for transfers between devices, body(): gathered = lax.all_gather(grad_out, 'row', axis=0, tiled=True)  77.8 us
    dot_general x1, matrix products, contract_last(): lax.dot_general(left_side, right_side, (((1,), (1,)), ((), ())), preferre...  14.3 us
  transfers between devices with their start and end apart: 2, of which 2 were waited for; matrix products, arithmetic and copies ran while one was open for 0% of the time, Pallas kernels for 0%

commit v1 on v0

--- a/solution.py
+++ b/solution.py
@@ -11,11 +11,12 @@
 
 
 def body(grad_out, weight):
+    n_col = lax.axis_size("col")
     gathered = lax.all_gather(grad_out, "row", axis=0, tiled=True)
-    rounded = lax.optimization_barrier(contract_last(gathered, weight).astype(jnp.bfloat16))
-    return lax.psum_scatter(
-        rounded.astype(jnp.float32).astype(jnp.bfloat16), "col", scatter_dimension=0, tiled=True
-    )
+    rounded = contract_last(gathered, weight).astype(jnp.bfloat16)
+    blocks = rounded.reshape(n_col, rounded.shape[0] // n_col, rounded.shape[1])
+    received = lax.all_to_all(blocks, "col", 0, 0, tiled=True)
+    return received.astype(jnp.float32).sum(0).astype(jnp.bfloat16)
 
 
 def solution(mesh):

time: 215 us -> 199 us (0.926)
  waiting for transfers between devices: 188 us -> 78.5 us
  blocking collectives: 0 us -> 90.2 us
  other arithmetic: 0 us -> 5.27 us
  matrix products: 14.3 us -> 11.3 us
    reduce_scatter x1 -> x0, waiting for transfers between devices: 109 us -> none  [body(): lax.psum_scatter(rounded.astype(jnp.float32).astype(jnp.bfloat16), 'col',...]
    all_to_all x0 -> x1, blocking collectives: none -> 90.2 us  [body(): received = lax.all_to_all(blocks, 'col', 0, 0, tiled=True)]
    reduce_sum x0 -> x1, other arithmetic: none -> 5.27 us  [body(): return received.astype(jnp.float32).sum(0).astype(jnp.bfloat16)]
    dot_general x1, matrix products: 14.3 us -> 11.3 us  [contract_last(): lax.dot_general(left_side, right_side, (((1,), (1,)), ((), ())), preferre...]
  transfers between devices with their start and end apart: 2 -> 1, of which waited for: 2 -> 1; matrix products, arithmetic and copies ran while one was open for 0% -> 0% of each run, Pallas kernels for 0% -> 0%
where the time goes in v1:
time: 199 us
  blocking collectives  90.2 us (45%)
  waiting for transfers between devices  78.5 us (39%)
  between operations  13.4 us (7%)
  matrix products  11.3 us (6%)
  other arithmetic  5.27 us (3%)
    all_to_all x1, blocking collectives, body(): received = lax.all_to_all(blocks, 'col', 0, 0, tiled=True)  90.2 us
    all_gather x1, waiting for transfers between devices, body(): gathered = lax.all_gather(grad_out, 'row', axis=0, tiled=True)  77.8 us
    dot_general x1, matrix products, contract_last(): lax.dot_general(left_side, right_side, (((1,), (1,)), ((), ())), preferre...  11.3 us
    reduce_sum x1, other arithmetic, body(): return received.astype(jnp.float32).sum(0).astype(jnp.bfloat16)  5.27 us
  transfers between devices with their start and end apart: 1, of which 1 were waited for; matrix products, arithmetic and copies ran while one was open for 0% of the time, Pallas kernels for 0%

profile of v1, /device:TPU:1, one launch (start us, length us, event | category | flops | bytes accessed | tf_op | source)
XLA Modules:
  0.0 198.8 jit_solution(12087622139959647830)
XLA Ops:
  6.5 0.0 copy-start
  6.5 0.0 all-gather.2.cloned.1.call-start
  6.5 0.7 all-gather.2.cloned.1.call-update
  7.3 77.8 %all-gather.2.cloned.1.call-done = bf16[4096,1024]{1,0:T(8,128)(2,1)} async-done(((bf16[128,1024]{1,0:T(8,128)(2,1)}), bf16[4096,1024]{1,0:T(8,128)(2,1)}) %all-gather.2.cloned.1.call-update) | async-done | bytes 8388624 | tf_op jit(solution)/shard_map/all_gather | solution.py:15
  85.1 0.0 copy-done
  85.1 11.3 %convolution_convert_fusion = bf16[4096,896]{1,0:T(8,128)(2,1)S(1)} fusion(bf16[4096,1024]{1,0:T(8,128)(2,1)} %all-gather.2.cloned.1.call-done, bf16[896,1024]{1,0:T(8,128)(2,1)S(1)} %copy-done), kind=kOutput, calls=%fused_computation | convolution fusion | flops 7519862784 | bytes 17563648 | tf_op jit(solution)/shard_map/dot_general | solution.py:8
  96.4 90.2 %all_to_all.5 = bf16[8,512,896]{2,1,0:T(8,128)(2,1)} all-to-all(bf16[8,512,896]{2,1,0:T(8,128)(2,1)S(1)} %bitcast.3), channel_id=1, replica_groups=mesh['row'=32,'col'=8] {'col'}, dimensions={0} | all-to-all | bytes 14680064 | tf_op jit(solution)/shard_map/all_to_all | solution.py:18
  186.7 5.3 %reduce_sum.12 = bf16[512,896]{1,0:T(8,128)(2,1)} reduce(bf16[8,512,896]{2,1,0:T(8,128)(2,1)} %all_to_all.5, bf16[]{:T(256)} %constant.2.clone.1), dimensions={0}, to_apply=%region_0.0 | reduce | flops 3211264 | bytes 8257538 | tf_op jit(solution)/shard_map/reduce_sum | solution.py:19
Async XLA Ops:
  6.5 78.6 %copy-start = (bf16[896,1024]{1,0:T(8,128)(2,1)S(1)}, bf16[896,1024]{1,0:T(8,128)(2,1)}, u32[]{:S(2)}) copy-start(bf16[896,1024]{1,0:T(8,128)(2,1)} %param.3) | copy-start | bytes 5505028
  6.5 78.6 %all-gather.2.cloned.1.call-start = ((), (), s32[]{:S(2)}) async-start(), calls=%async_computation.1 | async-start | bytes 8650752 | tf_op jit(solution)/shard_map/all_gather | solution.py:15
Sparse Core Ops, SparseCore 0:
  9.2 75.8 all-gather.1

commit v2 on v1

v2 whole, which is shorter than its diff:
```python
import jax
import jax.numpy as jnp
from jax import lax
from jax.sharding import Mesh, PartitionSpec as P


def contract_last(left_side, right_side):
    return lax.dot_general(
        left_side, right_side, (((1,), (1,)), ((), ())), preferred_element_type=jnp.float32
    )


def body(grad_out, weight):
    n_col = lax.axis_size("col")
    n_core = lax.axis_size("core")
    both = lax.all_gather(weight, "core", axis=0, tiled=True)
    gathered = lax.all_gather(grad_out, "rz", axis=0, tiled=True)
    rounded = contract_last(gathered, both).astype(jnp.bfloat16)
    blocks = rounded.reshape(n_col, rounded.shape[0] // n_col, rounded.shape[1])
    received = lax.all_to_all(blocks, "col", 0, 0, tiled=True)
    summed = received.astype(jnp.float32).sum(0).astype(jnp.bfloat16)
    rows, width = summed.shape[0], weight.shape[0]
    by_owner = summed.reshape(rows, n_core, width).transpose(1, 0, 2)
    mine = lax.all_to_all(by_owner, "core", 0, 0, tiled=True)
    per_row = grad_out.shape[0]
    mine = mine.reshape(n_core, rows // per_row, per_row, width).transpose(1, 0, 2, 3)
    return mine.reshape(-1, width)


def solution(mesh):
    n_row, n_col = mesh.devices.shape
    fine = Mesh(mesh.devices.reshape(n_row // 2, 2, n_col), ("rz", "core", "col"))
    in_specs = (P(("rz", "core"), "col"), P(("rz", "core"), "col"))
    out_specs = P("col", ("rz", "core"))
    return jax.shard_map(body, mesh=fine, in_specs=in_specs, out_specs=out_specs, check_vma=False)
```

time: 199 us -> 253 us (1.27)
  waiting for transfers between devices: 78.5 us -> 124 us
  blocking collectives: 90.2 us -> 97.5 us
    all_gather x1 -> x2, waiting for transfers between devices: 77.8 us -> 123 us  [the longest x1 99 us: body(): gathered = lax.all_gather(grad_out, 'rz', axis=0, tiled=True)]
    all_to_all x0 -> x1, blocking collectives: none -> 6.62 us  [body(): mine = lax.all_to_all(by_owner, 'core', 0, 0, tiled=True)]
  transfers between devices with their start and end apart: 1 -> 2, of which waited for: 1 -> 2; matrix products, arithmetic and copies ran while one was open for 0% -> 0% of each run, Pallas kernels for 0% -> 0%
where the time goes in v2:
time: 253 us
  waiting for transfers between devices  124 us (49%)
  blocking collectives  97.5 us (39%)
  between operations  13.4 us (5%)
  matrix products  10.7 us (4%)
  other arithmetic  4.59 us (2%)
    all_gather x1, waiting for transfers between devices, body(): gathered = lax.all_gather(grad_out, 'rz', axis=0, tiled=True)  99 us
    all_to_all x1, blocking collectives, body(): received = lax.all_to_all(blocks, 'col', 0, 0, tiled=True)  90.8 us
    all_gather x1, waiting for transfers between devices, body(): both = lax.all_gather(weight, 'core', axis=0, tiled=True)  23.9 us
    dot_general x1, matrix products, contract_last(): lax.dot_general(left_side, right_side, (((1,), (1,)), ((), ())), preferre...  10.7 us
    all_to_all x1, blocking collectives, body(): mine = lax.all_to_all(by_owner, 'core', 0, 0, tiled=True)  6.62 us
  transfers between devices with their start and end apart: 2, of which 2 were waited for; matrix products, arithmetic and copies ran while one was open for 0% of the time, Pallas kernels for 0%

profile of v2, /device:TPU:1, one launch (start us, length us, event | category | flops | bytes accessed | tf_op | source)
XLA Modules:
  0.0 252.7 jit_solution(3287596444993253392)
XLA Ops:
  6.5 0.0 all-gather.5.cloned.1.call-start
  6.5 0.7 all-gather.5.cloned.1.call-update
  7.3 0.0 all-gather.3.cloned.1.call-start
  7.3 0.7 all-gather.3.cloned.1.call-update
  8.0 23.9 %all-gather.5.cloned.1.call-done = bf16[1792,1024]{1,0:T(8,128)(2,1)} async-done(((bf16[896,1024]{1,0:T(8,128)(2,1)}), bf16[1792,1024]{1,0:T(8,128)(2,1)}) %all-gather.5.cloned.1.call-update) | async-done | bytes 3670032 | tf_op jit(solution)/shard_map/all_gather | solution.py:16
  31.9 99.0 %all-gather.3.cloned.1.call-done = bf16[2048,1024]{1,0:T(8,128)(2,1)} async-done(((bf16[128,1024]{1,0:T(8,128)(2,1)}), bf16[2048,1024]{1,0:T(8,128)(2,1)}) %all-gather.3.cloned.1.call-update) | async-done | bytes 4194320 | tf_op jit(solution)/shard_map/all_gather | solution.py:17
  131.0 10.7 %convolution_convert_fusion = bf16[2048,1792]{1,0:T(8,128)(2,1)S(1)} fusion(bf16[2048,1024]{1,0:T(8,128)(2,1)} %all-gather.3.cloned.1.call-done, bf16[1792,1024]{1,0:T(8,128)(2,1)} %all-gather.5.cloned.1.call-done), kind=kOutput, calls=%fused_computation | convolution fusion | flops 7519862784 | bytes 15204352 | tf_op jit(solution)/shard_map/dot_general | solution.py:8
  141.6 90.8 %all_to_all.10 = bf16[8,256,1792]{2,1,0:T(8,128)(2,1)} all-to-all(bf16[8,256,1792]{2,1,0:T(8,128)(2,1)S(1)} %bitcast.10), channel_id=1, replica_groups=mesh['rz'=16,'core'=2,'col'=8] {'col'}, dimensions={0} | all-to-all | bytes 14680064 | tf_op jit(solution)/shard_map/all_to_all | solution.py:20
  232.5 4.6 %reduce_sum.12 = bf16[256,1792]{1,0:T(8,128)(2,1)S(1)} reduce(bf16[8,256,1792]{2,1,0:T(8,128)(2,1)} %all_to_all.10, bf16[]{:T(256)} %constant.2.clone.1), dimensions={0}, to_apply=%region_0.0 | reduce | flops 3211264 | bytes 8257538 | tf_op jit(solution)/shard_map/reduce_sum | solution.py:21
  237.1 0.5 copy.5
  237.6 6.6 %all_to_all.11 = bf16[2,256,896]{1,2,0:T(8,128)(2,1)S(1)} all-to-all(bf16[2,256,896]{1,2,0:T(8,128)(2,1)S(1)} %bitcast.11), channel_id=1, replica_groups=mesh['rz'=16,'core'=2,'col'=8] {'core'}, dimensions={0} | all-to-all | bytes 1835008 | tf_op jit(solution)/shard_map/all_to_all | solution.py:24
  244.2 0.6 copy.6
  244.8 1.0 copy.7
Async XLA Ops:
  6.5 25.4 %all-gather.5.cloned.1.call-start = ((), (), s32[]{:S(2)}) async-start(), calls=%async_computation.3 | async-start | bytes 5505024 | tf_op jit(solution)/shard_map/all_gather | solution.py:16
  7.3 123.7 %all-gather.3.cloned.1.call-start = ((), (), s32[]{:S(2)}) async-start(), calls=%async_computation.2 | async-start | bytes 4456448 | tf_op jit(solution)/shard_map/all_gather | solution.py:17
Sparse Core Ops, SparseCore 0:
  9.1 22.7 all-gather.4
  33.7 97.2 all-gather.2
